TPU v7x, 512 devices: a whole 4x8x8 slice. The times are simulated.
512 devices in a mesh: grp: 4 (over x), gx: 16 (over z_hi, y), gy: 8 (over z_lo, core).
Axes of the slice: x: 4, y: 8, z: 8 (z_hi: 2, z_lo: 4; z = z_hi * 4 + z_lo), core: 2. Of those that a mesh axis runs over, the one named last changes fastest.
Arguments:
- fwd_now: float32 [3, 64, 64, 128], P(None, 'gx', 'gy'), may hold values from -6 to 6
- fwd_prev: float32 [3, 64, 64, 128], P(None, 'gx', 'gy'), may hold values from -6 to 6
- adj_now: float32 [16, 3, 64, 64, 128], P('grp', None, 'gx', 'gy'), may hold values from -6 to 6
- adj_prev: float32 [16, 3, 64, 64, 128], P('grp', None, 'gx', 'gy'), may hold values from -6 to 6
- lame_first: float32 [64, 64, 128], P('gx', 'gy'), may hold values from 0.5 to 2
- shear_mod: float32 [64, 64, 128], P('gx', 'gy'), may hold values from 0.3 to 1.2
- buoyancy: float32 [64, 64, 128], P('gx', 'gy'), may hold values from 0.5 to 1
- master_cell: int32 [1], replicated, may hold values from 0 to 524287
- master_lag: int32 [1], replicated, may hold values from 0 to 254
- master_trace: float32 [256, 3], replicated, may hold values from -96 to 96
- receiver_cell: int32 [16], P('grp'), may hold values from 0 to 524287
- receiver_lag: int32 [16], P('grp'), may hold values from 0 to 254
- receiver_trace: float32 [16, 256, 3], P('grp'), may hold values from -96 to 96
Outputs:
- adj_final: float32 [16, 3, 64, 64, 128], P('grp', None, 'gx', 'gy')
- kernels: float32 [2, 64, 64, 128], P(None, 'gx', 'gy', 'grp')
Inputs may be any that keep to these rules, and one draw needn't show every extreme that they name: `receiver_cell`: cell index in the whole grid, numbered (x * 64 + y) * 128 + z. `master_cell`: cell index in the whole grid, numbered (x * 64 + y) * 128 + z.
All inputs are finite; a program needn't handle non-finite values.
Results may differ from a plain program's by a relative error of at most 0.00011.
Values sent between devices are 32-bit elements; how exact they have to be, the bound alone decides.
No kernel may reach another device: no remote copies, remote signals or barrier semaphores. Data moves between devices by JAX's collectives and lax.ppermute only.
A program may use at most 64 MiB of HBM per device.

v0:
```python
import jax
import jax.numpy as jnp
from jax import lax
from jax.sharding import PartitionSpec as P

STEPS = 2
time_step_sq = 0.0625


def with_halo(cells, sides, width):
    for axis, dim in sides:
        count = lax.axis_size(axis)
        ends = count - 1
        head = lax.slice_in_dim(cells, 0, width, axis=dim)
        tail = lax.slice_in_dim(cells, cells.shape[dim] - width, cells.shape[dim], axis=dim)
        cells = jnp.concatenate(
            [
                lax.ppermute(tail, axis, [(i, (i + 1) % count) for i in range(ends)]),
                cells,
                lax.ppermute(head, axis, [((i + 1) % count, i) for i in range(ends)]),
            ],
            axis=dim,
        )
    return cells


def passed_along(value, axis, by):
    size = lax.axis_size(axis)
    pairs = [(i, i + by) for i in range(size) if 0 <= i + by < size]
    return lax.ppermute(value, axis, pairs)


def backward_diff(stress, axis):
    upper = stress[:, 1:, 1:, 1:]
    if axis == 1:
        lower = stress[:, :-1, 1:, 1:]
    elif axis == 2:
        lower = stress[:, 1:, :-1, 1:]
    else:
        lower = stress[:, 1:, 1:, :-1]
    return upper - lower


def stencil(padded, lame_pad, shear_pad):
    span_x = padded.shape[2] - 2
    span_y = padded.shape[3] - 2
    span_z = padded.shape[4] - 2
    anchor = padded[:, :, : span_x + 1, : span_y + 1, : span_z + 1]
    grad_x = padded[:, :, 1:, : span_y + 1, : span_z + 1] - anchor
    grad_y = padded[:, :, : span_x + 1, 1:, : span_z + 1] - anchor
    grad_z = padded[:, :, : span_x + 1, : span_y + 1, 1:] - anchor
    strain_xx = grad_x[:, 0]
    strain_yy = grad_y[:, 1]
    strain_zz = grad_z[:, 2]
    strain_xy = 0.5 * (grad_y[:, 0] + grad_x[:, 1])
    strain_xz = 0.5 * (grad_z[:, 0] + grad_x[:, 2])
    strain_yz = 0.5 * (grad_z[:, 1] + grad_y[:, 2])
    lame = lame_pad[: span_x + 1, : span_y + 1, : span_z + 1]
    shear = shear_pad[: span_x + 1, : span_y + 1, : span_z + 1]
    dilation = strain_xx + strain_yy + strain_zz
    stress_xx = lame * dilation + 2.0 * shear * strain_xx
    stress_yy = lame * dilation + 2.0 * shear * strain_yy
    stress_zz = lame * dilation + 2.0 * shear * strain_zz
    stress_xy = 2.0 * shear * strain_xy
    stress_xz = 2.0 * shear * strain_xz
    stress_yz = 2.0 * shear * strain_yz
    force_x = (
        backward_diff(stress_xx, 1) + backward_diff(stress_xy, 2) + backward_diff(stress_xz, 3)
    )
    force_y = (
        backward_diff(stress_xy, 1) + backward_diff(stress_yy, 2) + backward_diff(stress_yz, 3)
    )
    force_z = (
        backward_diff(stress_xz, 1) + backward_diff(stress_yz, 2) + backward_diff(stress_zz, 3)
    )
    force = jnp.stack([force_x, force_y, force_z], axis=1)
    strain = jnp.stack([strain_xx, strain_yy, strain_zz, strain_xy, strain_xz, strain_yz], axis=1)
    return (force, strain[:, :, 1:, 1:, 1:])


def faces(fields):
    count = fields.shape[0]
    flat = fields.reshape((count * 3,) + fields.shape[2:])
    grown = with_halo(flat, (("gx", 1), ("gy", 2)), 1)
    grown = jnp.pad(grown, ((0, 0), (0, 0), (0, 0), (1, 1)))
    return grown.reshape((count, 3) + grown.shape[1:])


def lower_rims(moduli):
    pairs, cells_x, cells_y, depth = moduli.shape
    from_x = passed_along(moduli[:, cells_x - 1 :], "gx", 1)
    from_y = passed_along(moduli[:, :, cells_y - 1 :], "gy", 1)
    corner = jnp.zeros((pairs, 1, 1, depth), jnp.float32)
    top_row = jnp.concatenate([corner, from_y], axis=1)
    rest = jnp.concatenate([from_x, moduli], axis=1)
    grown = jnp.concatenate([top_row, rest], axis=2)
    return jnp.pad(grown, ((0, 0), (0, 1), (0, 1), (1, 1)))


def locate(cells, start_x, start_y, start_z, width_y, depth, span_x, span_y, span_z):
    coord_x = cells // (width_y * depth) - start_x
    coord_y = cells // depth % width_y - start_y
    coord_z = cells % depth - start_z
    index_x = lax.broadcasted_iota(jnp.int32, (1, span_x, 1, 1), 1)
    index_y = lax.broadcasted_iota(jnp.int32, (1, 1, span_y, 1), 2)
    index_z = lax.broadcasted_iota(jnp.int32, (1, 1, 1, span_z), 3)
    found = (
        (index_x == coord_x[:, None, None, None])
        & (index_y == coord_y[:, None, None, None])
        & (index_z == coord_z[:, None, None, None])
    )
    return found.astype(jnp.float32)


def pick(trace, lags):
    positions = lax.broadcasted_iota(jnp.int32, (1, trace.shape[1]), 1)
    chosen = positions == lags[:, None]
    return jnp.sum(jnp.where(chosen[:, :, None], trace, 0.0), axis=1)


def advance(current, earlier, force, amplitudes, masks, buoyancy):
    source = amplitudes[:, :, None, None, None] * masks[:, None]
    return 2.0 * current - earlier + time_step_sq * buoyancy * (force + source)


def correlate(master, strains, totals):
    weights = jnp.array([1.0, 1.0, 1.0, 2.0, 2.0, 2.0], jnp.float32)[:, None, None, None]
    summed = jnp.sum(strains, axis=0)
    dilation_term = (master[0] + master[1] + master[2]) * (summed[0] + summed[1] + summed[2])
    shear_term = 2.0 * jnp.sum(weights * master * summed, axis=0)
    return totals + jnp.stack([dilation_term, shear_term])


def local(
    fwd_now,
    fwd_prev,
    adj_now,
    adj_prev,
    lame_first,
    shear_mod,
    buoyancy,
    master_cell,
    master_lag,
    master_trace,
    receiver_cell,
    receiver_lag,
    receiver_trace,
):
    cells_x, cells_y, depth = lame_first.shape
    groups = lax.axis_size("grp")
    receivers = adj_now.shape[0]
    width_y = cells_y * lax.axis_size("gy")
    start_x = lax.axis_index("gx") * cells_x
    start_y = lax.axis_index("gy") * cells_y
    moduli = lower_rims(jnp.stack([lame_first, shear_mod]))
    lame_pad = moduli[0]
    shear_pad = moduli[1]
    receiver_masks = locate(
        receiver_cell, start_x, start_y, 0, width_y, depth, cells_x, cells_y, depth
    )
    receiver_amps = [pick(receiver_trace, receiver_lag + instant) for instant in range(STEPS)]
    master_amps = [pick(master_trace[None], master_lag + instant) for instant in range(STEPS)]
    totals = jnp.zeros((2, cells_x, cells_y, depth), jnp.float32)
    share = depth // groups
    z_start = lax.axis_index("grp") * share
    master_now = lax.dynamic_slice_in_dim(fwd_now, z_start, share, 3)
    master_prev = lax.dynamic_slice_in_dim(fwd_prev, z_start, share, 3)
    lame_share = lax.dynamic_slice_in_dim(lame_pad, z_start, share + 2, 2)
    shear_share = lax.dynamic_slice_in_dim(shear_pad, z_start, share + 2, 2)
    buoyancy_share = lax.dynamic_slice_in_dim(buoyancy, z_start, share, 2)
    master_mask = locate(
        master_cell, start_x, start_y, z_start, width_y, depth, cells_x, cells_y, share
    )
    adjoint = adj_now
    adjoint_prev = adj_prev
    for instant in range(STEPS):
        grown = with_halo(master_now, (("grp", 3), ("gx", 1), ("gy", 2)), 1)
        master_force, master_strain = stencil(grown[None], lame_share, shear_share)
        master_whole = lax.all_gather(master_strain[0], "grp", axis=3, tiled=True)
        if instant + 1 < STEPS:
            master_next = advance(
                master_now[None],
                master_prev[None],
                master_force,
                master_amps[instant],
                master_mask,
                buoyancy_share,
            )[0]
            master_prev, master_now = (master_now, master_next)
        padded = faces(adjoint)
        force, strain = stencil(padded, lame_pad, shear_pad)
        totals = correlate(master_whole, strain, totals)
        adjoint_next = advance(
            adjoint, adjoint_prev, force, receiver_amps[instant], receiver_masks, buoyancy
        )
        adjoint_prev, adjoint = (adjoint, adjoint_next)
    scale_out = 1.0 / (STEPS * receivers * groups)
    kernels = lax.psum_scatter(totals * scale_out, "grp", scatter_dimension=3, tiled=True)
    return (adjoint, kernels)


def solution(mesh):
    in_specs = (
        P(None, "gx", "gy", None),
        P(None, "gx", "gy", None),
        P("grp", None, "gx", "gy", None),
        P("grp", None, "gx", "gy", None),
        P("gx", "gy", None),
        P("gx", "gy", None),
        P("gx", "gy", None),
        P(),
        P(),
        P(),
        P("grp"),
        P("grp"),
        P("grp", None, None),
    )
    out_specs = (P("grp", None, "gx", "gy", None), P(None, "gx", "gy", "grp"))
    return jax.shard_map(local, mesh=mesh, in_specs=in_specs, out_specs=out_specs, check_vma=False)
```

profile of v0, /device:TPU:8, one launch (start us, length us, event | category | flops | bytes accessed | tf_op | source)
XLA Modules:
  0.0 201.1 jit_solution(10094206814735372614)
XLA Ops:
  8.0 1.7 collective-permute-start
  9.7 3.5 %collective-permute-start.1 = (f32[2,1,8,128]{3,1,2,0:T(1,128)S(1)}, f32[2,1,8,128]{3,1,2,0:T(1,128)S(1)}, u32[]{:S(2)}, u32[]{:S(2)}) collective-permute-start(f32[2,1,8,128]{3,1,2,0:T(1,128)S(1)} %pad_maximum_fusion.14), channel_id=1, source_target_pairs={{0,8},{8,16},{16,24},{24,32},{32,40},{40,48},{48,56},{56,64},{64,7... | collective-permute-start | bytes 24584 | tf_op jit(solution)/shard_map/ppermute | solution.py:30
  14.2 3.4 %collective-permute-start.10 = (f32[3,4,8,1]{3,2,1,0:T(8,128)S(1)}, f32[3,4,8,1]{3,2,1,0:T(8,128)S(1)}, u32[]{:S(2)}, u32[]{:S(2)}) collective-permute-start(f32[3,4,8,1]{3,2,1,0:T(8,128)S(1)} %get-tuple-element.92), channel_id=1, source_target_pairs={{0,128},{128,256},{256,384},{1,129},{129,257},{257,385},{2,130},{1... | collective-permute-start | bytes 1160 | tf_op jit(solution)/shard_map/ppermute | solution.py:18
  17.6 1.3 collective-permute-start.11
  20.0 3.5 %collective-permute-start.2 = (f32[12,1,8,128]{3,1,2,0:T(1,128)S(1)}, f32[12,1,8,128]{3,1,2,0:T(1,128)S(1)}, u32[]{:S(2)}, u32[]{:S(2)}) collective-permute-start(f32[12,1,8,128]{3,1,2,0:T(1,128)S(1)} %get-tuple-element.66), channel_id=1, source_target_pairs={{0,8},{8,16},{16,24},{24,32},{32,40},{40,48},{48,56},{56,64},{64,7... | collective-permute-start | bytes 147464 | tf_op jit(solution)/shard_map/ppermute | solution.py:18
  30.8 4.7 %collective-permute-start.12 = (f32[3,1,8,34]{3,2,1,0:T(8,128)S(1)}, f32[3,1,8,34]{3,2,1,0:T(8,128)S(1)}, u32[]{:S(2)}, u32[]{:S(2)}) collective-permute-start(f32[3,1,8,34]{3,2,1,0:T(8,128)S(1)} %get-tuple-element.70), channel_id=1, source_target_pairs={{0,8},{8,16},{16,24},{24,32},{32,40},{40,48},{48,56},{56,64},{64,7... | collective-permute-start | bytes 9800 | tf_op jit(solution)/shard_map/ppermute | solution.py:18
  35.5 1.9 collective-permute-start.13
  37.4 3.6 %collective-permute-done.13 = f32[3,1,8,34]{3,2,1,0:T(8,128)S(1)} collective-permute-done((f32[3,1,8,34]{3,2,1,0:T(8,128)S(1)}, f32[3,1,8,34]{3,2,1,0:T(8,128)S(1)}, u32[]{:S(2)}, u32[]{:S(2)}) %collective-permute-start.13) | collective-permute-done | bytes 3296 | tf_op jit(solution)/shard_map/ppermute | solution.py:20
  41.2 2.4 %collective-permute-start.14 = (f32[3,6,1,34]{3,1,2,0:T(8,128)S(1)}, f32[3,6,1,34]{3,1,2,0:T(8,128)S(1)}, u32[]{:S(2)}, u32[]{:S(2)}) collective-permute-start(f32[3,6,1,34]{3,1,2,0:T(8,128)S(1)} %get-tuple-element.80), channel_id=1, source_target_pairs={{0,1},{1,2},{2,3},{3,4},{4,5},{5,6},{6,7},{8,9},{9,10},{10,11},{11... | collective-permute-start | bytes 7352 | tf_op jit(solution)/shard_map/ppermute | solution.py:18
  43.7 1.3 collective-permute-start.15
  45.1 2.2 %collective-permute-start.3 = (f32[12,1,8,128]{3,1,2,0:T(1,128)S(1)}, f32[12,1,8,128]{3,1,2,0:T(1,128)S(1)}, u32[]{:S(2)}, u32[]{:S(2)}) collective-permute-start(f32[12,1,8,128]{3,1,2,0:T(1,128)S(1)} %get-tuple-element.67), channel_id=1, source_target_pairs={{8,0},{16,8},{24,16},{32,24},{40,32},{48,40},{56,48},{64,56},{72,6... | collective-permute-start | bytes 147464 | tf_op jit(solution)/shard_map/ppermute | solution.py:20
  49.6 4.6 %collective-permute-start.16 = (f32[3,4,8,1]{3,2,1,0:T(8,128)S(1)}, f32[3,4,8,1]{3,2,1,0:T(8,128)S(1)}, u32[]{:S(2)}, u32[]{:S(2)}) collective-permute-start(f32[3,4,8,1]{3,2,1,0:T(8,128)S(1)} %get-tuple-element.90), channel_id=1, source_target_pairs={{0,128},{128,256},{256,384},{1,129},{129,257},{257,385},{2,130},{1... | collective-permute-start | bytes 1160 | tf_op jit(solution)/shard_map/ppermute | solution.py:18
  54.1 1.3 collective-permute-start.17
  55.9 4.3 %collective-permute-done.17 = f32[3,4,8,1]{3,2,1,0:T(8,128)S(1)} collective-permute-done((f32[3,4,8,1]{3,2,1,0:T(8,128)S(1)}, f32[3,4,8,1]{3,2,1,0:T(8,128)S(1)}, u32[]{:S(2)}, u32[]{:S(2)}) %collective-permute-start.17) | collective-permute-done | bytes 416 | tf_op jit(solution)/shard_map/ppermute | solution.py:20
  60.2 2.6 %collective-permute-start.18 = (f32[3,1,8,34]{3,2,1,0:T(8,128)S(1)}, f32[3,1,8,34]{3,2,1,0:T(8,128)S(1)}, u32[]{:S(2)}, u32[]{:S(2)}) collective-permute-start(f32[3,1,8,34]{3,2,1,0:T(8,128)S(1)} %get-tuple-element.68), channel_id=1, source_target_pairs={{0,8},{8,16},{16,24},{24,32},{32,40},{40,48},{48,56},{56,64},{64,7... | collective-permute-start | bytes 9800 | tf_op jit(solution)/shard_map/ppermute | solution.py:18
  62.8 3.3 %collective-permute-start.19 = (f32[3,1,8,34]{3,2,1,0:T(8,128)S(1)}, f32[3,1,8,34]{3,2,1,0:T(8,128)S(1)}, u32[]{:S(2)}, u32[]{:S(2)}) collective-permute-start(f32[3,1,8,34]{3,2,1,0:T(8,128)S(1)} %get-tuple-element.69), channel_id=1, source_target_pairs={{8,0},{16,8},{24,16},{32,24},{40,32},{48,40},{56,48},{64,56},{72,6... | collective-permute-start | bytes 9800 | tf_op jit(solution)/shard_map/ppermute | solution.py:20
  66.1 17.6 %all-gather = f32[1,6,4,8,128]{3,2,1,0,4:T(4,128)S(1)} all-gather(f32[1,6,4,8,32]{3,2,1,0,4:T(4,128)S(1)} %copy.434), channel_id=2, replica_groups=mesh['grp'=4,'gx'=16,'gy'=8] {'grp'}, dimensions={4}, use_global_device_ids=true | all-gather | bytes 122880 | tf_op jit(solution)/shard_map/all_gather | solution.py:179
  84.4 1.5 collective-permute-start.20
  85.9 1.3 collective-permute-start.21
  87.3 5.0 %collective-permute-done.21 = f32[3,6,1,34]{3,1,2,0:T(8,128)S(1)} collective-permute-done((f32[3,6,1,34]{3,1,2,0:T(8,128)S(1)}, f32[3,6,1,34]{3,1,2,0:T(8,128)S(1)}, u32[]{:S(2)}, u32[]{:S(2)}) %collective-permute-start.21) | collective-permute-done | bytes 2480 | tf_op jit(solution)/shard_map/ppermute | solution.py:20
  92.9 4.3 %collective-permute-start.4 = (f32[12,6,1,128]{3,1,2,0:T(8,128)S(1)}, f32[12,6,1,128]{3,1,2,0:T(8,128)S(1)}, u32[]{:S(2)}, u32[]{:S(2)}) collective-permute-start(f32[12,6,1,128]{3,1,2,0:T(8,128)S(1)} %get-tuple-element.59), channel_id=1, source_target_pairs={{0,1},{1,2},{2,3},{3,4},{4,5},{5,6},{6,7},{8,9},{9,10},{10,11},{11... | collective-permute-start | bytes 110600 | tf_op jit(solution)/shard_map/ppermute | solution.py:18
  97.3 1.3 collective-permute-start.5
  98.6 18.0 %all-gather.1 = f32[1,6,4,8,128]{3,2,1,0,4:T(4,128)S(1)} all-gather(f32[1,6,4,8,32]{3,2,1,0,4:T(4,128)S(1)} %copy.451), channel_id=3, replica_groups=mesh['grp'=4,'gx'=16,'gy'=8] {'grp'}, dimensions={4}, use_global_device_ids=true | all-gather | bytes 122880 | tf_op jit(solution)/shard_map/all_gather | solution.py:179
  116.6 1.2 copy.452
  120.7 3.5 %collective-permute-start.6 = (f32[12,1,8,128]{3,2,1,0:T(8,128)S(1)}, f32[12,1,8,128]{3,2,1,0:T(8,128)S(1)}, u32[]{:S(2)}, u32[]{:S(2)}) collective-permute-start(f32[12,1,8,128]{3,2,1,0:T(8,128)S(1)} %get-tuple-element.64), channel_id=1, source_target_pairs={{0,8},{8,16},{16,24},{24,32},{32,40},{40,48},{48,56},{56,64},{64,7... | collective-permute-start | bytes 147464 | tf_op jit(solution)/shard_map/ppermute | solution.py:18
  124.2 2.4 %collective-permute-start.7 = (f32[12,1,8,128]{3,2,1,0:T(8,128)S(1)}, f32[12,1,8,128]{3,2,1,0:T(8,128)S(1)}, u32[]{:S(2)}, u32[]{:S(2)}) collective-permute-start(f32[12,1,8,128]{3,2,1,0:T(8,128)S(1)} %get-tuple-element.65), channel_id=1, source_target_pairs={{8,0},{16,8},{24,16},{32,24},{40,32},{48,40},{56,48},{64,56},{72,6... | collective-permute-start | bytes 147464 | tf_op jit(solution)/shard_map/ppermute | solution.py:20
  127.2 4.8 %collective-permute-done.7 = f32[12,1,8,128]{3,2,1,0:T(8,128)S(1)} collective-permute-done((f32[12,1,8,128]{3,2,1,0:T(8,128)S(1)}, f32[12,1,8,128]{3,2,1,0:T(8,128)S(1)}, u32[]{:S(2)}, u32[]{:S(2)}) %collective-permute-start.7) | collective-permute-done | bytes 49184 | tf_op jit(solution)/shard_map/ppermute | solution.py:20
  132.0 1.3 collective-permute-start.8
  133.3 1.5 collective-permute-start.9
  134.8 3.6 %collective-permute-done.9 = f32[12,6,1,128]{3,2,1,0:T(1,128)S(1)} collective-permute-done((f32[12,6,1,128]{3,2,1,0:T(1,128)S(1)}, f32[12,6,1,128]{3,2,1,0:T(1,128)S(1)}, u32[]{:S(2)}, u32[]{:S(2)}) %collective-permute-start.9) | collective-permute-done | bytes 36896 | tf_op jit(solution)/shard_map/ppermute | solution.py:20
  139.7 2.0 %copy_subtract_fusion.1 = (f32[4,3,5,9,129]{4,2,3,0,1:T(8,128)S(1)}, f32[4,3,5,9,129]{4,2,3,0,1:T(8,128)S(1)}, f32[4,3,5,9,129]{4,2,3,0,1:T(8,128)S(1)}) fusion(f32[4,3,5,9,129]{4,3,2,1,0:T(8,128)S(1)} %get-tuple-element.34, f32[4,3,5,9,129]{4,3,2,1,0:T(8,128)S(1)} %get-tuple-element.35, f32[4,3,5,9,129]{4,3,2,1,0:T(8,128)S(1)} %get-tuple-element.37, ...), kind=kLoop, calls=%fused_computation.16 | loop fusion | flops 208980 | bytes 1950480 | tf_op jit(solution)/shard_map/sub | solution.py:50
  145.8 46.9 %reduce-scatter.4.cloned.1.call-done = f32[32,64]{1,0:T(8,128)} async-done(((f32[128,64]{1,0:T(8,128)}), f32[32,64]{1,0:T(8,128)}) %reduce-scatter.4.cloned.1.call-update) | async-done | bytes 8208
  (148 shorter events, 23.0 us)
Async XLA Ops:
  7.2 37.8 %copy-start.7 = (f32[256,3]{0,1:T(4,128)S(1)}, f32[256,3]{0,1:T(4,128)}, u32[]{:S(2)}) copy-start(f32[256,3]{0,1:T(4,128)} %param.24) | copy-start | bytes 9220
  7.2 185.5 %reduce-scatter.4.cloned.1.call-start = ((), (), s32[]{:S(2)}) async-start(), calls=%async_computation.1 | async-start | bytes 81920
  8.0 40.8 %collective-permute-start = (f32[2,4,1,128]{3,1,2,0:T(4,128)S(1)}, f32[2,4,1,128]{3,1,2,0:T(4,128)S(1)}, u32[]{:S(2)}, u32[]{:S(2)}) collective-permute-start(f32[2,4,1,128]{3,1,2,0:T(4,128)S(1)} %pad_maximum_fusion.15), channel_id=1, source_target_pairs={{0,1},{1,2},{2,3},{3,4},{4,5},{5,6},{6,7},{8,9},{9,10},{10,11},{11... | collective-permute-start | bytes 12296 | tf_op jit(solution)/shard_map/ppermute | solution.py:30
  9.7 39.0 %collective-permute-start.1 = (f32[2,1,8,128]{3,1,2,0:T(1,128)S(1)}, f32[2,1,8,128]{3,1,2,0:T(1,128)S(1)}, u32[]{:S(2)}, u32[]{:S(2)}) collective-permute-start(f32[2,1,8,128]{3,1,2,0:T(1,128)S(1)} %pad_maximum_fusion.14), channel_id=1, source_target_pairs={{0,8},{8,16},{16,24},{24,32},{32,40},{40,48},{48,56},{56,64},{64,7... | collective-permute-start | bytes 24584 | tf_op jit(solution)/shard_map/ppermute | solution.py:30
  14.2 16.5 %collective-permute-start.10 = (f32[3,4,8,1]{3,2,1,0:T(8,128)S(1)}, f32[3,4,8,1]{3,2,1,0:T(8,128)S(1)}, u32[]{:S(2)}, u32[]{:S(2)}) collective-permute-start(f32[3,4,8,1]{3,2,1,0:T(8,128)S(1)} %get-tuple-element.92), channel_id=1, source_target_pairs={{0,128},{128,256},{256,384},{1,129},{129,257},{257,385},{2,130},{1... | collective-permute-start | bytes 1160 | tf_op jit(solution)/shard_map/ppermute | solution.py:18
  17.6 13.1 %collective-permute-start.11 = (f32[3,4,8,1]{3,2,1,0:T(8,128)S(1)}, f32[3,4,8,1]{3,2,1,0:T(8,128)S(1)}, u32[]{:S(2)}, u32[]{:S(2)}) collective-permute-start(f32[3,4,8,1]{3,2,1,0:T(8,128)S(1)} %get-tuple-element.93), channel_id=1, source_target_pairs={{128,0},{256,128},{384,256},{129,1},{257,129},{385,257},{130,2},{2... | collective-permute-start | bytes 1160 | tf_op jit(solution)/shard_map/ppermute | solution.py:20
  20.0 72.9 %collective-permute-start.2 = (f32[12,1,8,128]{3,1,2,0:T(1,128)S(1)}, f32[12,1,8,128]{3,1,2,0:T(1,128)S(1)}, u32[]{:S(2)}, u32[]{:S(2)}) collective-permute-start(f32[12,1,8,128]{3,1,2,0:T(1,128)S(1)} %get-tuple-element.66), channel_id=1, source_target_pairs={{0,8},{8,16},{16,24},{24,32},{32,40},{40,48},{48,56},{56,64},{64,7... | collective-permute-start | bytes 147464 | tf_op jit(solution)/shard_map/ppermute | solution.py:18
  30.8 6.6 %collective-permute-start.12 = (f32[3,1,8,34]{3,2,1,0:T(8,128)S(1)}, f32[3,1,8,34]{3,2,1,0:T(8,128)S(1)}, u32[]{:S(2)}, u32[]{:S(2)}) collective-permute-start(f32[3,1,8,34]{3,2,1,0:T(8,128)S(1)} %get-tuple-element.70), channel_id=1, source_target_pairs={{0,8},{8,16},{16,24},{24,32},{32,40},{40,48},{48,56},{56,64},{64,7... | collective-permute-start | bytes 9800 | tf_op jit(solution)/shard_map/ppermute | solution.py:18
  35.5 5.6 %collective-permute-start.13 = (f32[3,1,8,34]{3,2,1,0:T(8,128)S(1)}, f32[3,1,8,34]{3,2,1,0:T(8,128)S(1)}, u32[]{:S(2)}, u32[]{:S(2)}) collective-permute-start(f32[3,1,8,34]{3,2,1,0:T(8,128)S(1)} %get-tuple-element.71), channel_id=1, source_target_pairs={{8,0},{16,8},{24,16},{32,24},{40,32},{48,40},{56,48},{64,56},{72,6... | collective-permute-start | bytes 9800 | tf_op jit(solution)/shard_map/ppermute | solution.py:20
  41.2 8.2 %copy-start.1 = (f32[3,4,8,128]{3,2,1,0:T(8,128)S(1)}, f32[3,4,8,128]{3,2,1,0:T(8,128)}, u32[]{:S(2)}) copy-start(f32[3,4,8,128]{3,2,1,0:T(8,128)} %param.15) | copy-start | bytes 147460
  41.2 8.2 %copy-start.6 = (f32[3,4,8,128]{3,2,1,0:T(8,128)S(1)}, f32[3,4,8,128]{3,2,1,0:T(8,128)}, u32[]{:S(2)}) copy-start(f32[3,4,8,128]{3,2,1,0:T(8,128)} %param.16) | copy-start | bytes 147460
  41.2 3.9 %collective-permute-start.14 = (f32[3,6,1,34]{3,1,2,0:T(8,128)S(1)}, f32[3,6,1,34]{3,1,2,0:T(8,128)S(1)}, u32[]{:S(2)}, u32[]{:S(2)}) collective-permute-start(f32[3,6,1,34]{3,1,2,0:T(8,128)S(1)} %get-tuple-element.80), channel_id=1, source_target_pairs={{0,1},{1,2},{2,3},{3,4},{4,5},{5,6},{6,7},{8,9},{9,10},{10,11},{11... | collective-permute-start | bytes 7352 | tf_op jit(solution)/shard_map/ppermute | solution.py:18
  43.7 4.9 %collective-permute-start.15 = (f32[3,6,1,34]{3,1,2,0:T(8,128)S(1)}, f32[3,6,1,34]{3,1,2,0:T(8,128)S(1)}, u32[]{:S(2)}, u32[]{:S(2)}) collective-permute-start(f32[3,6,1,34]{3,1,2,0:T(8,128)S(1)} %get-tuple-element.81), channel_id=1, source_target_pairs={{1,0},{2,1},{3,2},{4,3},{5,4},{6,5},{7,6},{9,8},{10,9},{11,10},{12... | collective-permute-start | bytes 7352 | tf_op jit(solution)/shard_map/ppermute | solution.py:20
  45.1 47.8 %collective-permute-start.3 = (f32[12,1,8,128]{3,1,2,0:T(1,128)S(1)}, f32[12,1,8,128]{3,1,2,0:T(1,128)S(1)}, u32[]{:S(2)}, u32[]{:S(2)}) collective-permute-start(f32[12,1,8,128]{3,1,2,0:T(1,128)S(1)} %get-tuple-element.67), channel_id=1, source_target_pairs={{8,0},{16,8},{24,16},{32,24},{40,32},{48,40},{56,48},{64,56},{72,6... | collective-permute-start | bytes 147464 | tf_op jit(solution)/shard_map/ppermute | solution.py:20
  49.6 6.3 %collective-permute-start.16 = (f32[3,4,8,1]{3,2,1,0:T(8,128)S(1)}, f32[3,4,8,1]{3,2,1,0:T(8,128)S(1)}, u32[]{:S(2)}, u32[]{:S(2)}) collective-permute-start(f32[3,4,8,1]{3,2,1,0:T(8,128)S(1)} %get-tuple-element.90), channel_id=1, source_target_pairs={{0,128},{128,256},{256,384},{1,129},{129,257},{257,385},{2,130},{1... | collective-permute-start | bytes 1160 | tf_op jit(solution)/shard_map/ppermute | solution.py:18
  54.1 6.0 %collective-permute-start.17 = (f32[3,4,8,1]{3,2,1,0:T(8,128)S(1)}, f32[3,4,8,1]{3,2,1,0:T(8,128)S(1)}, u32[]{:S(2)}, u32[]{:S(2)}) collective-permute-start(f32[3,4,8,1]{3,2,1,0:T(8,128)S(1)} %get-tuple-element.91), channel_id=1, source_target_pairs={{128,0},{256,128},{384,256},{129,1},{257,129},{385,257},{130,2},{2... | collective-permute-start | bytes 1160 | tf_op jit(solution)/shard_map/ppermute | solution.py:20
  60.2 24.1 %collective-permute-start.18 = (f32[3,1,8,34]{3,2,1,0:T(8,128)S(1)}, f32[3,1,8,34]{3,2,1,0:T(8,128)S(1)}, u32[]{:S(2)}, u32[]{:S(2)}) collective-permute-start(f32[3,1,8,34]{3,2,1,0:T(8,128)S(1)} %get-tuple-element.68), channel_id=1, source_target_pairs={{0,8},{8,16},{16,24},{24,32},{32,40},{40,48},{48,56},{56,64},{64,7... | collective-permute-start | bytes 9800 | tf_op jit(solution)/shard_map/ppermute | solution.py:18
  62.8 21.5 %collective-permute-start.19 = (f32[3,1,8,34]{3,2,1,0:T(8,128)S(1)}, f32[3,1,8,34]{3,2,1,0:T(8,128)S(1)}, u32[]{:S(2)}, u32[]{:S(2)}) collective-permute-start(f32[3,1,8,34]{3,2,1,0:T(8,128)S(1)} %get-tuple-element.69), channel_id=1, source_target_pairs={{8,0},{16,8},{24,16},{32,24},{40,32},{48,40},{56,48},{64,56},{72,6... | collective-permute-start | bytes 9800 | tf_op jit(solution)/shard_map/ppermute | solution.py:20
  84.3 50.5 %copy-start.2 = (f32[1,6,4,8,128]{4,2,3,1,0:T(4,128)}, f32[1,6,4,8,128]{4,2,3,1,0:T(4,128)S(1)}, u32[]{:S(2)}) copy-start(f32[1,6,4,8,128]{4,2,3,1,0:T(4,128)S(1)} %copy.435) | copy-start | bytes 294916
  84.4 2.8 %collective-permute-start.20 = (f32[3,6,1,34]{3,1,2,0:T(8,128)S(1)}, f32[3,6,1,34]{3,1,2,0:T(8,128)S(1)}, u32[]{:S(2)}, u32[]{:S(2)}) collective-permute-start(f32[3,6,1,34]{3,1,2,0:T(8,128)S(1)} %get-tuple-element.78), channel_id=1, source_target_pairs={{0,1},{1,2},{2,3},{3,4},{4,5},{5,6},{6,7},{8,9},{9,10},{10,11},{11... | collective-permute-start | bytes 7352 | tf_op jit(solution)/shard_map/ppermute | solution.py:18
  85.9 6.4 %collective-permute-start.21 = (f32[3,6,1,34]{3,1,2,0:T(8,128)S(1)}, f32[3,6,1,34]{3,1,2,0:T(8,128)S(1)}, u32[]{:S(2)}, u32[]{:S(2)}) collective-permute-start(f32[3,6,1,34]{3,1,2,0:T(8,128)S(1)} %get-tuple-element.79), channel_id=1, source_target_pairs={{1,0},{2,1},{3,2},{4,3},{5,4},{6,5},{7,6},{9,8},{10,9},{11,10},{12... | collective-permute-start | bytes 7352 | tf_op jit(solution)/shard_map/ppermute | solution.py:20
  92.9 24.9 %collective-permute-start.4 = (f32[12,6,1,128]{3,1,2,0:T(8,128)S(1)}, f32[12,6,1,128]{3,1,2,0:T(8,128)S(1)}, u32[]{:S(2)}, u32[]{:S(2)}) collective-permute-start(f32[12,6,1,128]{3,1,2,0:T(8,128)S(1)} %get-tuple-element.59), channel_id=1, source_target_pairs={{0,1},{1,2},{2,3},{3,4},{4,5},{5,6},{6,7},{8,9},{9,10},{10,11},{11... | collective-permute-start | bytes 110600 | tf_op jit(solution)/shard_map/ppermute | solution.py:18
  97.3 20.6 %collective-permute-start.5 = (f32[12,6,1,128]{3,1,2,0:T(8,128)S(1)}, f32[12,6,1,128]{3,1,2,0:T(8,128)S(1)}, u32[]{:S(2)}, u32[]{:S(2)}) collective-permute-start(f32[12,6,1,128]{3,1,2,0:T(8,128)S(1)} %get-tuple-element.60), channel_id=1, source_target_pairs={{1,0},{2,1},{3,2},{4,3},{5,4},{6,5},{7,6},{9,8},{10,9},{11,10},{12... | collective-permute-start | bytes 110600 | tf_op jit(solution)/shard_map/ppermute | solution.py:20
  119.5 0.9 copy-start
  119.5 1.0 copy-start.5
  120.7 6.5 %collective-permute-start.6 = (f32[12,1,8,128]{3,2,1,0:T(8,128)S(1)}, f32[12,1,8,128]{3,2,1,0:T(8,128)S(1)}, u32[]{:S(2)}, u32[]{:S(2)}) collective-permute-start(f32[12,1,8,128]{3,2,1,0:T(8,128)S(1)} %get-tuple-element.64), channel_id=1, source_target_pairs={{0,8},{8,16},{16,24},{24,32},{32,40},{40,48},{48,56},{56,64},{64,7... | collective-permute-start | bytes 147464 | tf_op jit(solution)/shard_map/ppermute | solution.py:18
  124.2 7.8 %collective-permute-start.7 = (f32[12,1,8,128]{3,2,1,0:T(8,128)S(1)}, f32[12,1,8,128]{3,2,1,0:T(8,128)S(1)}, u32[]{:S(2)}, u32[]{:S(2)}) collective-permute-start(f32[12,1,8,128]{3,2,1,0:T(8,128)S(1)} %get-tuple-element.65), channel_id=1, source_target_pairs={{8,0},{16,8},{24,16},{32,24},{40,32},{48,40},{56,48},{64,56},{72,6... | collective-permute-start | bytes 147464 | tf_op jit(solution)/shard_map/ppermute | solution.py:20
  132.0 2.8 %collective-permute-start.8 = (f32[12,6,1,128]{3,2,1,0:T(1,128)S(1)}, f32[12,6,1,128]{3,2,1,0:T(1,128)S(1)}, u32[]{:S(2)}, u32[]{:S(2)}) collective-permute-start(f32[12,6,1,128]{3,2,1,0:T(1,128)S(1)} %get-tuple-element.54), channel_id=1, source_target_pairs={{0,1},{1,2},{2,3},{3,4},{4,5},{5,6},{6,7},{8,9},{9,10},{10,11},{11... | collective-permute-start | bytes 110600 | tf_op jit(solution)/shard_map/ppermute | solution.py:18
  133.3 5.1 %collective-permute-start.9 = (f32[12,6,1,128]{3,2,1,0:T(1,128)S(1)}, f32[12,6,1,128]{3,2,1,0:T(1,128)S(1)}, u32[]{:S(2)}, u32[]{:S(2)}) collective-permute-start(f32[12,6,1,128]{3,2,1,0:T(1,128)S(1)} %get-tuple-element.55), channel_id=1, source_target_pairs={{1,0},{2,1},{3,2},{4,3},{5,4},{6,5},{7,6},{9,8},{10,9},{11,10},{12... | collective-permute-start | bytes 110600 | tf_op jit(solution)/shard_map/ppermute | solution.py:20
  142.0 0.9 copy-start.4
  142.1 0.9 copy-start.3
  142.1 0.9 copy-start.8
Sparse Core Ops, SparseCore 0:
  144.6 48.0 reduce-scatter.3
where the time goes:
time: 202 us; the launch traced here: 201 us
  waiting for transfers between devices  69.5 us (34%)
  starting transfers between devices  54.6 us (27%)
  blocking collectives  35.6 us (18%)
  between operations  16.4 us (8%)
  other arithmetic  13.2 us (7%)
  local copies, waits for them, and re-layouts  11.7 us (6%)
    unnamed x2, waiting for transfers between devices  46.9 us
    all_gather x2, blocking collectives, local(): master_whole = lax.all_gather(master_strain[0], 'grp', axis=3, tiled=True)  35.6 us
    ppermute x10, starting transfers between devices, with_halo(): lax.ppermute(tail, axis, [(i, (i + 1) % count) for i in range(ends)])  31.7 us
    ppermute x10, waiting for transfers between devices, with_halo(): lax.ppermute(head, axis, [((i + 1) % count, i) for i in range(ends)])  22.5 us
    ppermute x10, starting transfers between devices, with_halo(): lax.ppermute(head, axis, [((i + 1) % count, i) for i in range(ends)])  17.7 us
    unnamed x36, local copies, waits for them, and re-layouts  5.5 us
    ppermute x2, starting transfers between devices, passed_along(): return lax.ppermute(value, axis, pairs)  5.22 us
  transfers between devices with their start and end apart: 23, of which 8 were waited for; matrix products, arithmetic and copies ran while one was open for 7% of the time, Pallas kernels for 0%

commit v1 on v0

--- a/solution.py
+++ b/solution.py
@@ -176,7 +176,10 @@
     for instant in range(STEPS):
         grown = with_halo(master_now, (("grp", 3), ("gx", 1), ("gy", 2)), 1)
         master_force, master_strain = stencil(grown[None], lame_share, shear_share)
-        master_whole = lax.all_gather(master_strain[0], "grp", axis=3, tiled=True)
+        master_whole = jnp.concatenate(
+            lax.all_to_all(jnp.stack([master_strain[0]] * lax.axis_size("grp")), "grp", 0, 0),
+            axis=3,
+        )
         if instant + 1 < STEPS:
             master_next = advance(
                 master_now[None],

time: 202 us -> 181 us (0.90)
  blocking collectives: 35.6 us -> 0 us
  starting transfers between devices: 54.6 us -> 64.5 us
  other arithmetic: 13.2 us -> 17.6 us
    all_gather x2 -> x0, blocking collectives: 35.6 us -> none  [local(): master_whole = lax.all_gather(master_strain[0], 'grp', axis=3, tiled=True)]
    all_to_all x0 -> x2, starting transfers between devices: none -> 8.81 us  [local(): lax.all_to_all(jnp.stack([master_strain[0]] * lax.axis_size('grp')), 'grp...]
    ppermute x10, waiting for transfers between devices: 22.5 us -> 20.2 us  [with_halo(): lax.ppermute(head, axis, [((i + 1) % count, i) for i in range(ends)])]
    unnamed x36 -> x31, local copies, waits for them, and re-layouts: 5.5 us -> 7.11 us
  transfers between devices with their start and end apart: 23 -> 25, of which waited for: 8 -> 8; matrix products, arithmetic and copies ran while one was open for 7% -> 11% of each run, Pallas kernels for 0% -> 0%
where the time goes in v1:
time: 181 us; the launch traced here: 180 us
  waiting for transfers between devices  69.5 us (38%)
  starting transfers between devices  64.5 us (36%)
  other arithmetic  17.6 us (10%)
  between operations  16.4 us (9%)
  local copies, waits for them, and re-layouts  11.7 us (6%)
    unnamed x2, waiting for transfers between devices  48.9 us
    ppermute x10, starting transfers between devices, with_halo(): lax.ppermute(tail, axis, [(i, (i + 1) % count) for i in range(ends)])  33.1 us
    ppermute x10, waiting for transfers between devices, with_halo(): lax.ppermute(head, axis, [((i + 1) % count, i) for i in range(ends)])  20.2 us
    ppermute x10, starting transfers between devices, with_halo(): lax.ppermute(head, axis, [((i + 1) % count, i) for i in range(ends)])  17.3 us
    all_to_all x2, starting transfers between devices, local(): lax.all_to_all(jnp.stack([master_strain[0]] * lax.axis_size('grp')), 'grp...  8.81 us
    unnamed x31, local copies, waits for them, and re-layouts  7.11 us
    ppermute x2, starting transfers between devices, passed_along(): return lax.ppermute(value, axis, pairs)  5.22 us
  transfers between devices with their start and end apart: 25, of which 8 were waited for; matrix products, arithmetic and copies ran while one was open for 11% of the time, Pallas kernels for 0%

profile of v1, /device:TPU:8, one launch (start us, length us, event | category | flops | bytes accessed | tf_op | source)
XLA Modules:
  0.0 179.7 jit_solution(2158712157905923073)
XLA Ops:
  7.9 1.7 collective-permute-start
  9.7 3.5 %collective-permute-start.1 = (f32[2,1,8,128]{3,1,2,0:T(1,128)S(1)}, f32[2,1,8,128]{3,1,2,0:T(1,128)S(1)}, u32[]{:S(2)}, u32[]{:S(2)}) collective-permute-start(f32[2,1,8,128]{3,1,2,0:T(1,128)S(1)} %pad_maximum_fusion.22), channel_id=1, source_target_pairs={{0,8},{8,16},{16,24},{24,32},{32,40},{40,48},{48,56},{56,64},{64,7... | collective-permute-start | bytes 24584 | tf_op jit(solution)/shard_map/ppermute | solution.py:30
  14.2 3.4 %collective-permute-start.10 = (f32[3,4,8,1]{3,1,2,0:T(4,128)S(1)}, f32[3,4,8,1]{3,1,2,0:T(4,128)S(1)}, u32[]{:S(2)}, u32[]{:S(2)}) collective-permute-start(f32[3,4,8,1]{3,1,2,0:T(4,128)S(1)} %get-tuple-element.88), channel_id=1, source_target_pairs={{0,128},{128,256},{256,384},{1,129},{129,257},{257,385},{2,130},{1... | collective-permute-start | bytes 1160 | tf_op jit(solution)/shard_map/ppermute | solution.py:18
  17.6 1.3 collective-permute-start.11
  20.0 3.5 %collective-permute-start.2 = (f32[12,1,8,128]{3,1,2,0:T(1,128)S(1)}, f32[12,1,8,128]{3,1,2,0:T(1,128)S(1)}, u32[]{:S(2)}, u32[]{:S(2)}) collective-permute-start(f32[12,1,8,128]{3,1,2,0:T(1,128)S(1)} %get-tuple-element.62), channel_id=1, source_target_pairs={{0,8},{8,16},{16,24},{24,32},{32,40},{40,48},{48,56},{56,64},{64,7... | collective-permute-start | bytes 147464 | tf_op jit(solution)/shard_map/ppermute | solution.py:18
  30.0 4.7 %collective-permute-start.12 = (f32[3,1,8,34]{3,1,2,0:T(1,128)S(1)}, f32[3,1,8,34]{3,1,2,0:T(1,128)S(1)}, u32[]{:S(2)}, u32[]{:S(2)}) collective-permute-start(f32[3,1,8,34]{3,1,2,0:T(1,128)S(1)} %get-tuple-element.70), channel_id=1, source_target_pairs={{0,8},{8,16},{16,24},{24,32},{32,40},{40,48},{48,56},{56,64},{64,7... | collective-permute-start | bytes 9800 | tf_op jit(solution)/shard_map/ppermute | solution.py:18
  34.8 1.9 %collective-permute-start.13 = (f32[3,1,8,34]{3,1,2,0:T(1,128)S(1)}, f32[3,1,8,34]{3,1,2,0:T(1,128)S(1)}, u32[]{:S(2)}, u32[]{:S(2)}) collective-permute-start(f32[3,1,8,34]{3,1,2,0:T(1,128)S(1)} %get-tuple-element.71), channel_id=1, source_target_pairs={{8,0},{16,8},{24,16},{32,24},{40,32},{48,40},{56,48},{64,56},{72,6... | collective-permute-start | bytes 9800 | tf_op jit(solution)/shard_map/ppermute | solution.py:20
  36.7 3.6 %collective-permute-done.13 = f32[3,1,8,34]{3,1,2,0:T(1,128)S(1)} collective-permute-done((f32[3,1,8,34]{3,1,2,0:T(1,128)S(1)}, f32[3,1,8,34]{3,1,2,0:T(1,128)S(1)}, u32[]{:S(2)}, u32[]{:S(2)}) %collective-permute-start.13) | collective-permute-done | bytes 3296 | tf_op jit(solution)/shard_map/ppermute | solution.py:20
  40.4 2.3 %collective-permute-start.14 = (f32[3,6,1,34]{3,1,2,0:T(8,128)S(1)}, f32[3,6,1,34]{3,1,2,0:T(8,128)S(1)}, u32[]{:S(2)}, u32[]{:S(2)}) collective-permute-start(f32[3,6,1,34]{3,1,2,0:T(8,128)S(1)} %get-tuple-element.66), channel_id=1, source_target_pairs={{0,1},{1,2},{2,3},{3,4},{4,5},{5,6},{6,7},{8,9},{9,10},{10,11},{11... | collective-permute-start | bytes 7352 | tf_op jit(solution)/shard_map/ppermute | solution.py:18
  42.7 1.3 collective-permute-start.15
  44.2 2.2 %collective-permute-start.3 = (f32[12,1,8,128]{3,1,2,0:T(1,128)S(1)}, f32[12,1,8,128]{3,1,2,0:T(1,128)S(1)}, u32[]{:S(2)}, u32[]{:S(2)}) collective-permute-start(f32[12,1,8,128]{3,1,2,0:T(1,128)S(1)} %get-tuple-element.63), channel_id=1, source_target_pairs={{8,0},{16,8},{24,16},{32,24},{40,32},{48,40},{56,48},{64,56},{72,6... | collective-permute-start | bytes 147464 | tf_op jit(solution)/shard_map/ppermute | solution.py:20
  48.7 4.6 %collective-permute-start.16 = (f32[3,4,8,1]{3,1,2,0:T(4,128)S(1)}, f32[3,4,8,1]{3,1,2,0:T(4,128)S(1)}, u32[]{:S(2)}, u32[]{:S(2)}) collective-permute-start(f32[3,4,8,1]{3,1,2,0:T(4,128)S(1)} %get-tuple-element.86), channel_id=1, source_target_pairs={{0,128},{128,256},{256,384},{1,129},{129,257},{257,385},{2,130},{1... | collective-permute-start | bytes 1160 | tf_op jit(solution)/shard_map/ppermute | solution.py:18
  53.2 1.3 collective-permute-start.17
  55.0 4.3 %collective-permute-done.17 = f32[3,4,8,1]{3,1,2,0:T(4,128)S(1)} collective-permute-done((f32[3,4,8,1]{3,1,2,0:T(4,128)S(1)}, f32[3,4,8,1]{3,1,2,0:T(4,128)S(1)}, u32[]{:S(2)}, u32[]{:S(2)}) %collective-permute-start.17) | collective-permute-done | bytes 416 | tf_op jit(solution)/shard_map/ppermute | solution.py:20
  59.4 2.6 %collective-permute-start.18 = (f32[3,1,8,34]{3,1,2,0:T(1,128)S(1)}, f32[3,1,8,34]{3,1,2,0:T(1,128)S(1)}, u32[]{:S(2)}, u32[]{:S(2)}) collective-permute-start(f32[3,1,8,34]{3,1,2,0:T(1,128)S(1)} %get-tuple-element.68), channel_id=1, source_target_pairs={{0,8},{8,16},{16,24},{24,32},{32,40},{40,48},{48,56},{56,64},{64,7... | collective-permute-start | bytes 9800 | tf_op jit(solution)/shard_map/ppermute | solution.py:18
  62.0 3.3 %collective-permute-start.19 = (f32[3,1,8,34]{3,1,2,0:T(1,128)S(1)}, f32[3,1,8,34]{3,1,2,0:T(1,128)S(1)}, u32[]{:S(2)}, u32[]{:S(2)}) collective-permute-start(f32[3,1,8,34]{3,1,2,0:T(1,128)S(1)} %get-tuple-element.69), channel_id=1, source_target_pairs={{8,0},{16,8},{24,16},{32,24},{40,32},{48,40},{56,48},{64,56},{72,6... | collective-permute-start | bytes 9800 | tf_op jit(solution)/shard_map/ppermute | solution.py:20
  66.3 4.0 %all-to-all-start = ((f32[4,1,6144]{2,1,0:T(1,128)}), f32[4,1,6144]{2,1,0:T(1,128)S(1)}, u32[]{:S(2)}, u32[]{:S(2)}) async-start(f32[4,1,6144]{2,1,0:T(1,128)} %reshape.447), calls=%async_computation | async-start | bytes 196608 | tf_op jit(solution)/shard_map/all_to_all | solution.py:180
  70.4 2.1 %collective-permute-start.20 = (f32[3,6,1,34]{3,1,2,0:T(8,128)S(1)}, f32[3,6,1,34]{3,1,2,0:T(8,128)S(1)}, u32[]{:S(2)}, u32[]{:S(2)}) collective-permute-start(f32[3,6,1,34]{3,1,2,0:T(8,128)S(1)} %get-tuple-element.64), channel_id=1, source_target_pairs={{0,1},{1,2},{2,3},{3,4},{4,5},{5,6},{6,7},{8,9},{9,10},{10,11},{11... | collective-permute-start | bytes 7352 | tf_op jit(solution)/shard_map/ppermute | solution.py:18
  72.5 1.3 collective-permute-start.21
  73.8 4.4 %collective-permute-done.21 = f32[3,6,1,34]{3,1,2,0:T(8,128)S(1)} collective-permute-done((f32[3,6,1,34]{3,1,2,0:T(8,128)S(1)}, f32[3,6,1,34]{3,1,2,0:T(8,128)S(1)}, u32[]{:S(2)}, u32[]{:S(2)}) %collective-permute-start.21) | collective-permute-done | bytes 2480 | tf_op jit(solution)/shard_map/ppermute | solution.py:20
  79.5 4.3 %collective-permute-start.4 = (f32[12,6,1,128]{3,1,2,0:T(8,128)S(1)}, f32[12,6,1,128]{3,1,2,0:T(8,128)S(1)}, u32[]{:S(2)}, u32[]{:S(2)}) collective-permute-start(f32[12,6,1,128]{3,1,2,0:T(8,128)S(1)} %get-tuple-element.55), channel_id=1, source_target_pairs={{0,1},{1,2},{2,3},{3,4},{4,5},{5,6},{6,7},{8,9},{9,10},{10,11},{11... | collective-permute-start | bytes 110600 | tf_op jit(solution)/shard_map/ppermute | solution.py:18
  83.9 1.3 collective-permute-start.5
  85.2 4.8 %all-to-all-start.1 = ((f32[4,1,6144]{2,1,0:T(1,128)}), f32[4,1,6144]{2,1,0:T(1,128)S(1)}, u32[]{:S(2)}, u32[]{:S(2)}) async-start(f32[4,1,6144]{2,1,0:T(1,128)} %reshape.445), calls=%async_computation.1 | async-start | bytes 196608 | tf_op jit(solution)/shard_map/all_to_all | solution.py:180
  94.6 3.8 %collective-permute-start.6 = (f32[12,1,8,128]{3,2,1,0:T(8,128)S(1)}, f32[12,1,8,128]{3,2,1,0:T(8,128)S(1)}, u32[]{:S(2)}, u32[]{:S(2)}) collective-permute-start(f32[12,1,8,128]{3,2,1,0:T(8,128)S(1)} %get-tuple-element.60), channel_id=1, source_target_pairs={{0,8},{8,16},{16,24},{24,32},{32,40},{40,48},{48,56},{56,64},{64,7... | collective-permute-start | bytes 147464 | tf_op jit(solution)/shard_map/ppermute | solution.py:18
  98.5 2.0 %collective-permute-start.7 = (f32[12,1,8,128]{3,2,1,0:T(8,128)S(1)}, f32[12,1,8,128]{3,2,1,0:T(8,128)S(1)}, u32[]{:S(2)}, u32[]{:S(2)}) collective-permute-start(f32[12,1,8,128]{3,2,1,0:T(8,128)S(1)} %get-tuple-element.61), channel_id=1, source_target_pairs={{8,0},{16,8},{24,16},{32,24},{40,32},{48,40},{56,48},{64,56},{72,6... | collective-permute-start | bytes 147464 | tf_op jit(solution)/shard_map/ppermute | solution.py:20
  102.4 3.8 %collective-permute-done.7 = f32[12,1,8,128]{3,2,1,0:T(8,128)S(1)} collective-permute-done((f32[12,1,8,128]{3,2,1,0:T(8,128)S(1)}, f32[12,1,8,128]{3,2,1,0:T(8,128)S(1)}, u32[]{:S(2)}, u32[]{:S(2)}) %collective-permute-start.7) | collective-permute-done | bytes 49184 | tf_op jit(solution)/shard_map/ppermute | solution.py:20
  106.3 1.9 %collective-permute-start.8 = (f32[12,6,1,128]{3,2,1,0:T(1,128)S(1)}, f32[12,6,1,128]{3,2,1,0:T(1,128)S(1)}, u32[]{:S(2)}, u32[]{:S(2)}) collective-permute-start(f32[12,6,1,128]{3,2,1,0:T(1,128)S(1)} %get-tuple-element.50), channel_id=1, source_target_pairs={{0,1},{1,2},{2,3},{3,4},{4,5},{5,6},{6,7},{8,9},{9,10},{10,11},{11... | collective-permute-start | bytes 110600 | tf_op jit(solution)/shard_map/ppermute | solution.py:18
  108.2 1.5 collective-permute-start.9
  109.9 2.9 %collective-permute-done.9 = f32[12,6,1,128]{3,2,1,0:T(1,128)S(1)} collective-permute-done((f32[12,6,1,128]{3,2,1,0:T(1,128)S(1)}, f32[12,6,1,128]{3,2,1,0:T(1,128)S(1)}, u32[]{:S(2)}, u32[]{:S(2)}) %collective-permute-start.9) | collective-permute-done | bytes 36896 | tf_op jit(solution)/shard_map/ppermute | solution.py:20
  114.0 2.0 %copy_subtract_fusion.1 = (f32[4,3,5,9,129]{4,2,3,0,1:T(8,128)S(1)}, f32[4,3,5,9,129]{4,2,3,0,1:T(8,128)S(1)}, f32[4,3,5,9,129]{4,2,3,0,1:T(8,128)S(1)}) fusion(f32[4,3,5,9,129]{4,3,2,1,0:T(8,128)S(1)} %get-tuple-element.30, f32[4,3,5,9,129]{4,3,2,1,0:T(8,128)S(1)} %get-tuple-element.31, f32[4,3,5,9,129]{4,3,2,1,0:T(8,128)S(1)} %get-tuple-element.33, ...), kind=kLoop, calls=%fused_computation.16 | loop fusion | flops 208980 | bytes 1950480 | tf_op jit(solution)/shard_map/sub | solution.py:50
  120.0 1.6 fusion.31
  122.4 48.8 %reduce-scatter.4.cloned.1.call-done = f32[32,64]{1,0:T(8,128)} async-done(((f32[128,64]{1,0:T(8,128)}), f32[32,64]{1,0:T(8,128)}) %reduce-scatter.4.cloned.1.call-update) | async-done | bytes 8208
  (154 shorter events, 27.4 us)
Async XLA Ops:
  7.2 36.9 %copy-start.2 = (f32[256,3]{0,1:T(4,128)S(1)}, f32[256,3]{0,1:T(4,128)}, u32[]{:S(2)}) copy-start(f32[256,3]{0,1:T(4,128)} %param.24) | copy-start | bytes 9220
  7.9 39.9 %collective-permute-start = (f32[2,4,1,128]{3,1,2,0:T(4,128)S(1)}, f32[2,4,1,128]{3,1,2,0:T(4,128)S(1)}, u32[]{:S(2)}, u32[]{:S(2)}) collective-permute-start(f32[2,4,1,128]{3,1,2,0:T(4,128)S(1)} %pad_maximum_fusion.23), channel_id=1, source_target_pairs={{0,1},{1,2},{2,3},{3,4},{4,5},{5,6},{6,7},{8,9},{9,10},{10,11},{11... | collective-permute-start | bytes 12296 | tf_op jit(solution)/shard_map/ppermute | solution.py:30
  9.7 38.2 %collective-permute-start.1 = (f32[2,1,8,128]{3,1,2,0:T(1,128)S(1)}, f32[2,1,8,128]{3,1,2,0:T(1,128)S(1)}, u32[]{:S(2)}, u32[]{:S(2)}) collective-permute-start(f32[2,1,8,128]{3,1,2,0:T(1,128)S(1)} %pad_maximum_fusion.22), channel_id=1, source_target_pairs={{0,8},{8,16},{16,24},{24,32},{32,40},{40,48},{48,56},{56,64},{64,7... | collective-permute-start | bytes 24584 | tf_op jit(solution)/shard_map/ppermute | solution.py:30
  14.2 15.6 %collective-permute-start.10 = (f32[3,4,8,1]{3,1,2,0:T(4,128)S(1)}, f32[3,4,8,1]{3,1,2,0:T(4,128)S(1)}, u32[]{:S(2)}, u32[]{:S(2)}) collective-permute-start(f32[3,4,8,1]{3,1,2,0:T(4,128)S(1)} %get-tuple-element.88), channel_id=1, source_target_pairs={{0,128},{128,256},{256,384},{1,129},{129,257},{257,385},{2,130},{1... | collective-permute-start | bytes 1160 | tf_op jit(solution)/shard_map/ppermute | solution.py:18
  17.6 12.2 %collective-permute-start.11 = (f32[3,4,8,1]{3,1,2,0:T(4,128)S(1)}, f32[3,4,8,1]{3,1,2,0:T(4,128)S(1)}, u32[]{:S(2)}, u32[]{:S(2)}) collective-permute-start(f32[3,4,8,1]{3,1,2,0:T(4,128)S(1)} %get-tuple-element.89), channel_id=1, source_target_pairs={{128,0},{256,128},{384,256},{129,1},{257,129},{385,257},{130,2},{2... | collective-permute-start | bytes 1160 | tf_op jit(solution)/shard_map/ppermute | solution.py:20
  20.0 59.5 %collective-permute-start.2 = (f32[12,1,8,128]{3,1,2,0:T(1,128)S(1)}, f32[12,1,8,128]{3,1,2,0:T(1,128)S(1)}, u32[]{:S(2)}, u32[]{:S(2)}) collective-permute-start(f32[12,1,8,128]{3,1,2,0:T(1,128)S(1)} %get-tuple-element.62), channel_id=1, source_target_pairs={{0,8},{8,16},{16,24},{24,32},{32,40},{40,48},{48,56},{56,64},{64,7... | collective-permute-start | bytes 147464 | tf_op jit(solution)/shard_map/ppermute | solution.py:18
  30.0 6.6 %collective-permute-start.12 = (f32[3,1,8,34]{3,1,2,0:T(1,128)S(1)}, f32[3,1,8,34]{3,1,2,0:T(1,128)S(1)}, u32[]{:S(2)}, u32[]{:S(2)}) collective-permute-start(f32[3,1,8,34]{3,1,2,0:T(1,128)S(1)} %get-tuple-element.70), channel_id=1, source_target_pairs={{0,8},{8,16},{16,24},{24,32},{32,40},{40,48},{48,56},{56,64},{64,7... | collective-permute-start | bytes 9800 | tf_op jit(solution)/shard_map/ppermute | solution.py:18
  34.8 5.6 %collective-permute-start.13 = (f32[3,1,8,34]{3,1,2,0:T(1,128)S(1)}, f32[3,1,8,34]{3,1,2,0:T(1,128)S(1)}, u32[]{:S(2)}, u32[]{:S(2)}) collective-permute-start(f32[3,1,8,34]{3,1,2,0:T(1,128)S(1)} %get-tuple-element.71), channel_id=1, source_target_pairs={{8,0},{16,8},{24,16},{32,24},{40,32},{48,40},{56,48},{64,56},{72,6... | collective-permute-start | bytes 9800 | tf_op jit(solution)/shard_map/ppermute | solution.py:20
  40.4 3.7 %collective-permute-start.14 = (f32[3,6,1,34]{3,1,2,0:T(8,128)S(1)}, f32[3,6,1,34]{3,1,2,0:T(8,128)S(1)}, u32[]{:S(2)}, u32[]{:S(2)}) collective-permute-start(f32[3,6,1,34]{3,1,2,0:T(8,128)S(1)} %get-tuple-element.66), channel_id=1, source_target_pairs={{0,1},{1,2},{2,3},{3,4},{4,5},{5,6},{6,7},{8,9},{9,10},{10,11},{11... | collective-permute-start | bytes 7352 | tf_op jit(solution)/shard_map/ppermute | solution.py:18
  42.7 4.9 %collective-permute-start.15 = (f32[3,6,1,34]{3,1,2,0:T(8,128)S(1)}, f32[3,6,1,34]{3,1,2,0:T(8,128)S(1)}, u32[]{:S(2)}, u32[]{:S(2)}) collective-permute-start(f32[3,6,1,34]{3,1,2,0:T(8,128)S(1)} %get-tuple-element.67), channel_id=1, source_target_pairs={{1,0},{2,1},{3,2},{4,3},{5,4},{6,5},{7,6},{9,8},{10,9},{11,10},{12... | collective-permute-start | bytes 7352 | tf_op jit(solution)/shard_map/ppermute | solution.py:20
  44.2 35.3 %collective-permute-start.3 = (f32[12,1,8,128]{3,1,2,0:T(1,128)S(1)}, f32[12,1,8,128]{3,1,2,0:T(1,128)S(1)}, u32[]{:S(2)}, u32[]{:S(2)}) collective-permute-start(f32[12,1,8,128]{3,1,2,0:T(1,128)S(1)} %get-tuple-element.63), channel_id=1, source_target_pairs={{8,0},{16,8},{24,16},{32,24},{40,32},{48,40},{56,48},{64,56},{72,6... | collective-permute-start | bytes 147464 | tf_op jit(solution)/shard_map/ppermute | solution.py:20
  48.7 6.3 %collective-permute-start.16 = (f32[3,4,8,1]{3,1,2,0:T(4,128)S(1)}, f32[3,4,8,1]{3,1,2,0:T(4,128)S(1)}, u32[]{:S(2)}, u32[]{:S(2)}) collective-permute-start(f32[3,4,8,1]{3,1,2,0:T(4,128)S(1)} %get-tuple-element.86), channel_id=1, source_target_pairs={{0,128},{128,256},{256,384},{1,129},{129,257},{257,385},{2,130},{1... | collective-permute-start | bytes 1160 | tf_op jit(solution)/shard_map/ppermute | solution.py:18
  53.2 6.0 %collective-permute-start.17 = (f32[3,4,8,1]{3,1,2,0:T(4,128)S(1)}, f32[3,4,8,1]{3,1,2,0:T(4,128)S(1)}, u32[]{:S(2)}, u32[]{:S(2)}) collective-permute-start(f32[3,4,8,1]{3,1,2,0:T(4,128)S(1)} %get-tuple-element.87), channel_id=1, source_target_pairs={{128,0},{256,128},{384,256},{129,1},{257,129},{385,257},{130,2},{2... | collective-permute-start | bytes 1160 | tf_op jit(solution)/shard_map/ppermute | solution.py:20
  59.4 10.9 %collective-permute-start.18 = (f32[3,1,8,34]{3,1,2,0:T(1,128)S(1)}, f32[3,1,8,34]{3,1,2,0:T(1,128)S(1)}, u32[]{:S(2)}, u32[]{:S(2)}) collective-permute-start(f32[3,1,8,34]{3,1,2,0:T(1,128)S(1)} %get-tuple-element.68), channel_id=1, source_target_pairs={{0,8},{8,16},{16,24},{24,32},{32,40},{40,48},{48,56},{56,64},{64,7... | collective-permute-start | bytes 9800 | tf_op jit(solution)/shard_map/ppermute | solution.py:18
  62.0 8.3 %collective-permute-start.19 = (f32[3,1,8,34]{3,1,2,0:T(1,128)S(1)}, f32[3,1,8,34]{3,1,2,0:T(1,128)S(1)}, u32[]{:S(2)}, u32[]{:S(2)}) collective-permute-start(f32[3,1,8,34]{3,1,2,0:T(1,128)S(1)} %get-tuple-element.69), channel_id=1, source_target_pairs={{8,0},{16,8},{24,16},{32,24},{40,32},{48,40},{56,48},{64,56},{72,6... | collective-permute-start | bytes 9800 | tf_op jit(solution)/shard_map/ppermute | solution.py:20
  66.3 18.9 %all-to-all-start = ((f32[4,1,6144]{2,1,0:T(1,128)}), f32[4,1,6144]{2,1,0:T(1,128)S(1)}, u32[]{:S(2)}, u32[]{:S(2)}) async-start(f32[4,1,6144]{2,1,0:T(1,128)} %reshape.447), calls=%async_computation | async-start | bytes 196608 | tf_op jit(solution)/shard_map/all_to_all | solution.py:180
  70.4 3.4 %collective-permute-start.20 = (f32[3,6,1,34]{3,1,2,0:T(8,128)S(1)}, f32[3,6,1,34]{3,1,2,0:T(8,128)S(1)}, u32[]{:S(2)}, u32[]{:S(2)}) collective-permute-start(f32[3,6,1,34]{3,1,2,0:T(8,128)S(1)} %get-tuple-element.64), channel_id=1, source_target_pairs={{0,1},{1,2},{2,3},{3,4},{4,5},{5,6},{6,7},{8,9},{9,10},{10,11},{11... | collective-permute-start | bytes 7352 | tf_op jit(solution)/shard_map/ppermute | solution.py:18
  72.5 5.7 %collective-permute-start.21 = (f32[3,6,1,34]{3,1,2,0:T(8,128)S(1)}, f32[3,6,1,34]{3,1,2,0:T(8,128)S(1)}, u32[]{:S(2)}, u32[]{:S(2)}) collective-permute-start(f32[3,6,1,34]{3,1,2,0:T(8,128)S(1)} %get-tuple-element.65), channel_id=1, source_target_pairs={{1,0},{2,1},{3,2},{4,3},{5,4},{6,5},{7,6},{9,8},{10,9},{11,10},{12... | collective-permute-start | bytes 7352 | tf_op jit(solution)/shard_map/ppermute | solution.py:20
  79.5 12.2 %collective-permute-start.4 = (f32[12,6,1,128]{3,1,2,0:T(8,128)S(1)}, f32[12,6,1,128]{3,1,2,0:T(8,128)S(1)}, u32[]{:S(2)}, u32[]{:S(2)}) collective-permute-start(f32[12,6,1,128]{3,1,2,0:T(8,128)S(1)} %get-tuple-element.55), channel_id=1, source_target_pairs={{0,1},{1,2},{2,3},{3,4},{4,5},{5,6},{6,7},{8,9},{9,10},{10,11},{11... | collective-permute-start | bytes 110600 | tf_op jit(solution)/shard_map/ppermute | solution.py:18
  83.9 7.9 %collective-permute-start.5 = (f32[12,6,1,128]{3,1,2,0:T(8,128)S(1)}, f32[12,6,1,128]{3,1,2,0:T(8,128)S(1)}, u32[]{:S(2)}, u32[]{:S(2)}) collective-permute-start(f32[12,6,1,128]{3,1,2,0:T(8,128)S(1)} %get-tuple-element.56), channel_id=1, source_target_pairs={{1,0},{2,1},{3,2},{4,3},{5,4},{6,5},{7,6},{9,8},{10,9},{11,10},{12... | collective-permute-start | bytes 110600 | tf_op jit(solution)/shard_map/ppermute | solution.py:20
  85.2 16.1 %all-to-all-start.1 = ((f32[4,1,6144]{2,1,0:T(1,128)}), f32[4,1,6144]{2,1,0:T(1,128)S(1)}, u32[]{:S(2)}, u32[]{:S(2)}) async-start(f32[4,1,6144]{2,1,0:T(1,128)} %reshape.445), calls=%async_computation.1 | async-start | bytes 196608 | tf_op jit(solution)/shard_map/all_to_all | solution.py:180
  90.0 81.3 %reduce-scatter.4.cloned.1.call-start = ((), (), s32[]{:S(2)}) async-start(), calls=%async_computation.3 | async-start | bytes 81920
  93.4 0.9 copy-start
  93.4 1.0 copy-start.1
  94.6 7.8 %collective-permute-start.6 = (f32[12,1,8,128]{3,2,1,0:T(8,128)S(1)}, f32[12,1,8,128]{3,2,1,0:T(8,128)S(1)}, u32[]{:S(2)}, u32[]{:S(2)}) collective-permute-start(f32[12,1,8,128]{3,2,1,0:T(8,128)S(1)} %get-tuple-element.60), channel_id=1, source_target_pairs={{0,8},{8,16},{16,24},{24,32},{32,40},{40,48},{48,56},{56,64},{64,7... | collective-permute-start | bytes 147464 | tf_op jit(solution)/shard_map/ppermute | solution.py:18
  98.5 7.8 %collective-permute-start.7 = (f32[12,1,8,128]{3,2,1,0:T(8,128)S(1)}, f32[12,1,8,128]{3,2,1,0:T(8,128)S(1)}, u32[]{:S(2)}, u32[]{:S(2)}) collective-permute-start(f32[12,1,8,128]{3,2,1,0:T(8,128)S(1)} %get-tuple-element.61), channel_id=1, source_target_pairs={{8,0},{16,8},{24,16},{32,24},{40,32},{48,40},{56,48},{64,56},{72,6... | collective-permute-start | bytes 147464 | tf_op jit(solution)/shard_map/ppermute | solution.py:20
  106.3 3.6 %collective-permute-start.8 = (f32[12,6,1,128]{3,2,1,0:T(1,128)S(1)}, f32[12,6,1,128]{3,2,1,0:T(1,128)S(1)}, u32[]{:S(2)}, u32[]{:S(2)}) collective-permute-start(f32[12,6,1,128]{3,2,1,0:T(1,128)S(1)} %get-tuple-element.50), channel_id=1, source_target_pairs={{0,1},{1,2},{2,3},{3,4},{4,5},{5,6},{6,7},{8,9},{9,10},{10,11},{11... | collective-permute-start | bytes 110600 | tf_op jit(solution)/shard_map/ppermute | solution.py:18
  108.2 4.6 %collective-permute-start.9 = (f32[12,6,1,128]{3,2,1,0:T(1,128)S(1)}, f32[12,6,1,128]{3,2,1,0:T(1,128)S(1)}, u32[]{:S(2)}, u32[]{:S(2)}) collective-permute-start(f32[12,6,1,128]{3,2,1,0:T(1,128)S(1)} %get-tuple-element.51), channel_id=1, source_target_pairs={{1,0},{2,1},{3,2},{4,3},{5,4},{6,5},{7,6},{9,8},{10,9},{11,10},{12... | collective-permute-start | bytes 110600 | tf_op jit(solution)/shard_map/ppermute | solution.py:20
  117.2 0.8 copy-start.3
Sparse Core Ops, SparseCore 0:
  120.1 51.1 reduce-scatter.3
